TPU v7x, 512 devices: a whole 4x4x16 slice. The times are simulated.
512 devices in a mesh: dp: 64 (over y, z), tensor: 8 (over x, core).
Axes of the slice: x: 4, y: 4, z: 16, core: 2. Of those that a mesh axis runs over, the one named last changes fastest.
Arguments:
- tokens: bfloat16 [65536, 1408], P(('dp', 'tensor')), may hold values from -6 to 6
- ln1_gain: float32 [1408], replicated, may hold values from 0.1 to 1.9
- ln1_shift: float32 [1408], replicated, may hold values from -3 to 3
- w_qkv: bfloat16 [1408, 16, 264], P(None, 'tensor')
- w_out: bfloat16 [16, 88, 1408], P('tensor'), may hold values from -0.625 to 0.625
- ln2_gain: float32 [1408], replicated, may hold values from 0.1 to 1.9
- ln2_shift: float32 [1408], replicated, may hold values from -3 to 3
- w_proj: bfloat16 [5632, 3584], P('dp', 'tensor'), may hold values from -0.078125 to 0.078125
- proj_bias: float32 [3584], P('tensor'), may hold values from -3 to 3
- segments: int32 [64, 256], P('dp'), may hold values from 0 to 7, never falling along the last dimension, each value on 1 to 128 neighbouring positions
- owners: int32 [16384, 1], P('dp'), may hold values from 0 to 63; in each aligned block of 256 rows (0 to 255, 256 to 511, ...) at most 8 rows name the same one
Outputs:
- delivered: bfloat16 [32768, 3584], P('dp', 'tensor')
Inputs may be any that keep to these rules, and one draw needn't show every extreme that they name: `segments`: within a pack numbers never fall, every image has 1 to 128 groups and one has exactly that many. `owners`: among the 256 merged tokens of one pack no owner gets more than 8; in some pack an owner gets exactly 8.
All inputs are finite; a program needn't handle non-finite values.
Results may differ from a plain program's by a relative error of at most 0.015.
Values may be sent and summed in bfloat16 or wider, within the bound.
No kernel may reach another device: no remote copies, remote signals or barrier semaphores. Data moves between devices by JAX's collectives and lax.ppermute only.
A program may use at most 64 MiB of HBM per device.

v0:
```python
import jax
import jax.numpy as jnp
from jax import lax
from jax.sharding import PartitionSpec as P


def layer_norm(values, gain, shift):
    wide = values.astype(jnp.float32)
    average = jnp.mean(wide, axis=-1, keepdims=True)
    centred = wide - average
    variance = jnp.mean(centred * centred, axis=-1, keepdims=True)
    return centred * lax.rsqrt(variance + 1e-06) * gain + shift


def attend(heads_qkv, token_segs):
    row_count = heads_qkv.shape[0]
    width = heads_qkv.shape[2] // 3
    queries = heads_qkv[:, :, :width]
    keys_all = heads_qkv[:, :, width : 2 * width]
    values_all = heads_qkv[:, :, 2 * width :]
    score_scale = 1.0 / jnp.sqrt(jnp.float32(width))
    block_rows = min(512, row_count)
    outputs = []
    for block_index in range(row_count // block_rows):
        lower = block_index * block_rows
        scores = (
            jnp.einsum(
                "qhd,khd->hqk",
                queries[lower : lower + block_rows],
                keys_all,
                preferred_element_type=jnp.float32,
            )
            * score_scale
        )
        same = token_segs[lower : lower + block_rows][:, None] == token_segs[None, :]
        scores = jnp.where(same[None], scores, -jnp.inf)
        row_max = jnp.max(scores, axis=-1, keepdims=True)
        exponent = jnp.exp(scores - row_max)
        probs = (exponent / jnp.sum(exponent, axis=-1, keepdims=True)).astype(jnp.bfloat16)
        context = jnp.einsum("hqk,khd->qhd", probs, values_all, preferred_element_type=jnp.float32)
        outputs.append(context.astype(jnp.bfloat16))
    return jnp.concatenate(outputs, axis=0)


def shards(
    tokens,
    ln1_gain,
    ln1_shift,
    w_qkv,
    w_out,
    ln2_gain,
    ln2_shift,
    w_proj,
    proj_bias,
    segments,
    owners,
):
    dp_count = lax.axis_size("dp")
    tp_count = lax.axis_size("tensor")
    w_proj_all = lax.all_gather(w_proj, "dp", axis=0, tiled=True)
    w_out_all = lax.all_gather(w_out, "tensor", axis=0, tiled=True)
    gathered = lax.all_gather(tokens, "tensor", axis=0, tiled=True)
    row_count = gathered.shape[0]
    local_rows = tokens.shape[0]
    normed = layer_norm(gathered, ln1_gain, ln1_shift).astype(jnp.bfloat16)
    heads_here = w_qkv.shape[1]
    heads_qkv = jnp.dot(
        normed, w_qkv.reshape(w_qkv.shape[0], -1), preferred_element_type=jnp.float32
    )
    heads_qkv = heads_qkv.astype(jnp.bfloat16).reshape(row_count, heads_here, -1)
    token_segs = jnp.repeat(segments[0], 4)
    context = attend(heads_qkv, token_segs).reshape(tp_count, local_rows, -1)
    context_mine = lax.all_to_all(context, "tensor", split_axis=0, concat_axis=0, tiled=True)
    out_heads = w_out_all.reshape(tp_count, -1, w_out_all.shape[2])
    attn = jnp.einsum("sqd,sdo->qo", context_mine, out_heads, preferred_element_type=jnp.float32)
    hidden = (tokens.astype(jnp.float32) + attn).astype(jnp.bfloat16)
    normed_two = layer_norm(hidden, ln2_gain, ln2_shift).astype(jnp.bfloat16)
    merged_mine = normed_two.reshape(local_rows // 4, -1)
    merged = lax.all_gather(merged_mine, "tensor", axis=0, tiled=True)
    groups = merged.shape[0]
    summed = jnp.dot(merged, w_proj_all, preferred_element_type=jnp.float32)
    projected = (summed + proj_bias).astype(jnp.bfloat16)
    dests = owners[:, 0]
    onehot = (dests[:, None] == jnp.arange(dp_count, dtype=jnp.int32)[None, :]).astype(jnp.int32)
    earlier = jnp.cumsum(onehot, axis=0) - onehot
    position = jnp.sum(earlier * onehot, axis=1)
    capacity = 2 * groups // dp_count
    slot_index = dests * capacity + position
    scatter_table = (
        slot_index[None, :] == jnp.arange(dp_count * capacity, dtype=jnp.int32)[:, None]
    ).astype(jnp.bfloat16)
    outgoing = jnp.dot(scatter_table, projected, preferred_element_type=jnp.float32).astype(
        jnp.bfloat16
    )
    outgoing = outgoing.reshape(dp_count, capacity, -1)
    arrived = lax.all_to_all(outgoing, "dp", split_axis=0, concat_axis=0, tiled=True)
    return arrived.reshape(dp_count * capacity, -1)


def solution(mesh):
    return jax.shard_map(
        shards,
        mesh=mesh,
        in_specs=(
            P(("dp", "tensor"), None),
            P(),
            P(),
            P(None, "tensor", None),
            P("tensor", None, None),
            P(),
            P(),
            P("dp", "tensor"),
            P("tensor"),
            P("dp", None),
            P("dp", None),
        ),
        out_specs=P("dp", "tensor"),
        check_vma=False,
    )
```

profile of v0, /device:TPU:8, one launch (start us, length us, event | category | flops | bytes accessed | tf_op | source)
XLA Modules:
  0.0 339.7 jit_solution(10978495204272725188)
XLA Ops:
  6.5 0.0 copy-start
  6.5 0.0 copy-start.7
  6.5 0.0 copy-start.6
  6.5 0.0 all-gather.5.cloned.1.call-start
  6.5 0.7 all-gather.5.cloned.1.call-update
  7.3 0.0 all-gather.7.cloned.1.call-start
  7.3 0.7 all-gather.7.cloned.1.call-update
  8.0 0.0 all-gather.11.cloned.1.call-start
  8.1 0.7 all-gather.11.cloned.1.call-update
  8.7 0.0 all-gather.9.cloned.1.call-start
  8.8 0.7 slice_bitcast_fusion.1
  9.5 0.1 broadcast_in_dim.24
  9.5 0.1 eq.84
  9.7 0.1 broadcast_in_dim.28
  9.7 0.1 eq.89
  9.9 0.8 broadcast_in_dim.25
  10.6 0.1 eq.86
  10.8 0.7 broadcast_compare_fusion.1
  11.4 36.8 %all-gather.5.cloned.1.call-done = bf16[1024,1408]{1,0:T(8,128)(2,1)} async-done(((bf16[128,1408]{1,0:T(8,128)(2,1)}), bf16[1024,1408]{1,0:T(8,128)(2,1)}) %all-gather.5.cloned.1.call-update) | async-done | bytes 2883600 | tf_op jit(solution)/shard_map/all_gather | solution.py:62
  48.2 0.0 copy-start.1
  48.2 2.4 convert_reduce_fusion
  50.6 0.3 copy-done.1
  50.9 0.9 fusion.4
  51.8 0.0 copy-done
  51.8 0.0 copy-done.7
  51.8 0.0 copy-done.6
  51.8 3.1 fusion.27
  55.0 4.8 %fusion.82 = (f32[2,512]{1,0:T(2,128)S(1)}, f32[2,512,1024]{2,1,0:T(8,128)}) fusion(pred[512,1024]{1,0:T(8,128)(4,1)S(1)} %get-tuple-element.5, bf16[1024,2,264]{0,2,1:T(8,128)(2,1)} %bitcast.63), kind=kOutput, calls=%fused_computation.86 | convolution fusion | flops 188744704 | bytes 5263360 | tf_op jit(solution)/shard_map/sub | solution.py:38
  59.8 0.0 copy-start.9
  59.8 4.8 %fusion.73 = (f32[2,512]{1,0:T(2,128)S(1)}, f32[2,512,1024]{2,1,0:T(8,128)}) fusion(pred[512,1024]{1,0:T(8,128)(4,1)S(1)} %get-tuple-element.6, bf16[1024,2,264]{0,2,1:T(8,128)(2,1)} %bitcast.64), kind=kOutput, calls=%fused_computation.85 | convolution fusion | flops 188744704 | bytes 5263360 | tf_op jit(solution)/shard_map/sub | solution.py:38
  64.6 0.0 copy-done.9
  64.6 0.0 copy-start.10
  64.6 3.2 fusion.33
  67.8 0.4 copy-done.10
  68.2 0.0 copy-start.2
  68.2 0.9 fusion.34
  69.1 0.0 copy-start.4
  69.1 0.0 copy-start.5
  69.1 0.1 copy.22
  69.3 16.0 %all_to_all.10 = bf16[8,128,176]{1,2,0:T(8,128)(2,1)S(1)} all-to-all(bf16[8,128,176]{1,2,0:T(8,128)(2,1)S(1)} %copy.18), channel_id=1, replica_groups=mesh['dp'=64,'tensor'=8] {'tensor'}, dimensions={0} | all-to-all | bytes 720896 | tf_op jit(solution)/shard_map/all_to_all | solution.py:73
  85.2 0.0 copy-start.3
  85.2 8.4 %all-gather.7.cloned.1.call-done = bf16[16,88,1408]{2,1,0:T(8,128)(2,1)} async-done(((bf16[2,88,1408]{2,1,0:T(8,128)(2,1)}), bf16[16,88,1408]{2,1,0:T(8,128)(2,1)}) %all-gather.7.cloned.1.call-update) | async-done | bytes 3964944 | tf_op jit(solution)/shard_map/all_gather | solution.py:61
  93.6 0.0 copy-done.2
  93.7 0.0 copy-start.8
  93.7 3.0 fusion.91
  96.7 0.2 multiply_reduce_fusion
  96.9 0.0 copy-done.4
  96.9 0.0 copy-done.5
  96.9 0.2 add_convert_fusion
  97.1 1.0 reshape.155
  98.1 0.0 all-gather.9.cloned.1.call-update
  98.1 0.0 copy-done.3
  98.2 0.6 reduce-window.6
  98.8 0.2 slice_reduce_fusion
  99.0 0.1 fusion.67
  99.1 146.7 %all-gather.11.cloned.1.call-done = bf16[5632,448]{1,0:T(8,128)(2,1)} async-done(((bf16[88,448]{1,0:T(8,128)(2,1)}), bf16[5632,448]{1,0:T(8,128)(2,1)}) %all-gather.11.cloned.1.call-update) | async-done | bytes 5046288 | tf_op jit(solution)/shard_map/all_gather | solution.py:60
  245.8 32.5 %all-gather.9.cloned.1.call-done = bf16[256,5632]{1,0:T(8,128)(2,1)} async-done(((bf16[32,5632]{1,0:T(8,128)(2,1)}), bf16[256,5632]{1,0:T(8,128)(2,1)}) %all-gather.9.cloned.1.call-update) | async-done | bytes 2883600 | tf_op jit(solution)/shard_map/all_gather | solution.py:79
  278.3 0.0 copy-done.8
  278.3 6.0 %convolution_convert_fusion = bf16[512,448]{0,1:T(8,128)(2,1)S(1)} fusion(bf16[256,5632]{1,0:T(8,128)(2,1)} %all-gather.9.cloned.1.call-done, bf16[5632,448]{1,0:T(8,128)(2,1)} %all-gather.11.cloned.1.call-done, s32[256]{0:T(256)S(1)} %multiply_add_fusion, f32[448]{0:T(512)S(1)} %copy-done.8), kind=kOutput, calls=%fused_computation.36 | convolution fusion | flops 1409875968 | bytes 8391424 | tf_op jit(solution)/shard_map/dot_general | solution.py:92
  284.3 0.2 copy.19
  284.5 47.7 %all_to_all.11 = bf16[64,8,448]{2,1,0:T(8,128)(2,1)S(1)} all-to-all(bf16[64,8,448]{2,1,0:T(8,128)(2,1)S(1)} %bitcast.55), channel_id=1, replica_groups=mesh['dp'=64,'tensor'=8] {'dp'}, dimensions={0} | all-to-all | bytes 917504 | tf_op jit(solution)/shard_map/all_to_all | solution.py:96
  332.2 1.0 copy.20
  (10 shorter events, 0.2 us)
Async XLA Ops:
  6.5 45.3 %copy-start = (bf16[1408,2,264]{0,2,1:T(8,128)(2,1)S(1)}, bf16[1408,2,264]{0,2,1:T(8,128)(2,1)}, u32[]{:S(2)}) copy-start(bf16[1408,2,264]{0,2,1:T(8,128)(2,1)} %param.14) | copy-start | bytes 4460548
  6.5 45.3 %copy-start.7 = (f32[1408]{0:T(1024)S(1)}, f32[1408]{0:T(1024)}, u32[]{:S(2)}) copy-start(f32[1408]{0:T(1024)} %param.12) | copy-start | bytes 16900
  6.5 45.3 %copy-start.6 = (f32[1408]{0:T(1024)S(1)}, f32[1408]{0:T(1024)}, u32[]{:S(2)}) copy-start(f32[1408]{0:T(1024)} %param.13) | copy-start | bytes 16900
  6.5 41.7 %all-gather.5.cloned.1.call-start = ((), (), s32[]{:S(2)}) async-start(), calls=%async_computation.2 | async-start | bytes 3244032 | tf_op jit(solution)/shard_map/all_gather | solution.py:62
  7.3 86.4 %all-gather.7.cloned.1.call-start = ((), (), s32[]{:S(2)}) async-start(), calls=%async_computation.3 | async-start | bytes 4460544 | tf_op jit(solution)/shard_map/all_gather | solution.py:61
  8.0 237.8 %all-gather.11.cloned.1.call-start = ((), (), s32[]{:S(2)}) async-start(), calls=%async_computation.5 | async-start | bytes 5857280 | tf_op jit(solution)/shard_map/all_gather | solution.py:60
  8.7 269.5 %all-gather.9.cloned.1.call-start = ((), (), s32[]{:S(2)}) async-start(), calls=%async_computation.4 | async-start | bytes 3244032 | tf_op jit(solution)/shard_map/all_gather | solution.py:79
  48.2 2.7 copy-start.1
  59.8 4.8 %copy-start.9 = (bf16[1024,528]{0,1:T(8,128)(2,1)S(1)}, bf16[1024,528]{0,1:T(8,128)(2,1)}, u32[]{:S(2)}) copy-start(bf16[1024,528]{0,1:T(8,128)(2,1)} %fusion.27) | copy-start | bytes 3244036
  64.6 3.6 %copy-start.10 = (f32[2,512,1024]{2,1,0:T(8,128)S(1)}, f32[2,512,1024]{2,1,0:T(8,128)}, u32[]{:S(2)}) copy-start(f32[2,512,1024]{2,1,0:T(8,128)} %get-tuple-element.10) | copy-start | bytes 12582916
  68.2 25.5 %copy-start.2 = (bf16[128,1408]{1,0:T(8,128)(2,1)S(1)}, bf16[128,1408]{1,0:T(8,128)(2,1)}, u32[]{:S(2)}) copy-start(bf16[128,1408]{1,0:T(8,128)(2,1)} %param.11) | copy-start | bytes 1081348
  69.1 27.8 %copy-start.4 = (f32[1408]{0:T(1024)S(1)}, f32[1408]{0:T(1024)}, u32[]{:S(2)}) copy-start(f32[1408]{0:T(1024)} %param.17) | copy-start | bytes 16900
  69.1 27.8 %copy-start.5 = (f32[1408]{0:T(1024)S(1)}, f32[1408]{0:T(1024)}, u32[]{:S(2)}) copy-start(f32[1408]{0:T(1024)} %param.16) | copy-start | bytes 16900
  85.2 12.9 %copy-start.3 = (s32[256,1]{0,1:T(1,128)S(1)}, s32[256,1]{0,1:T(1,128)}, u32[]{:S(2)}) copy-start(s32[256,1]{0,1:T(1,128)} %param.21) | copy-start | bytes 3076
  93.7 184.6 %copy-start.8 = (f32[448]{0:T(512)S(1)}, f32[448]{0:T(512)}, u32[]{:S(2)}) copy-start(f32[448]{0:T(512)} %param.19) | copy-start | bytes 5380
Sparse Core Ops, SparseCore 0:
  9.5 38.6 all-gather.4
  50.3 43.2 all-gather.6
  96.6 149.1 all-gather.10
  247.8 30.4 all-gather.8
where the time goes:
time: 340 us
  waiting for transfers between devices  226 us (66%)
  blocking collectives  63.7 us (19%)
  matrix products  25.8 us (8%)
  between operations  13.3 us (4%)
  other arithmetic  5.21 us (2%)
  local copies, waits for them, and re-layouts  5.09 us (1%)
    all_gather x1, waiting for transfers between devices, shards(): w_proj_all = lax.all_gather(w_proj, 'dp', axis=0, tiled=True)  147 us
    all_to_all x1, blocking collectives, shards(): lax.all_to_all(outgoing, 'dp', split_axis=0, concat_axis=0, tiled=True)  47.7 us
    all_gather x1, waiting for transfers between devices, shards(): gathered = lax.all_gather(tokens, 'tensor', axis=0, tiled=True)  36.8 us
    all_gather x1, waiting for transfers between devices, shards(): merged = lax.all_gather(merged_mine, 'tensor', axis=0, tiled=True)  32.5 us
    all_to_all x1, blocking collectives, shards(): lax.all_to_all(context, 'tensor', split_axis=0, concat_axis=0, tiled=True)  16 us
    sub x2, matrix products, attend(): exponent = jnp.exp(scores - row_max)  9.62 us
    all_gather x1, waiting for transfers between devices, shards(): w_out_all = lax.all_gather(w_out, 'tensor', axis=0, tiled=True)  8.44 us
  transfers between devices with their start and end apart: 4, of which 4 were waited for; matrix products, arithmetic and copies ran while one was open for 8% of the time, Pallas kernels for 0%

commit v1 on v0

--- a/solution.py
+++ b/solution.py
@@ -2,6 +2,28 @@
 import jax.numpy as jnp
 from jax import lax
 from jax.sharding import PartitionSpec as P
+
+
+def joined_along(blocks, dim):
+    blocks = jnp.moveaxis(blocks, 0, dim)
+    shape = blocks.shape
+    return blocks.reshape(*shape[:dim], shape[dim] * shape[dim + 1], *shape[dim + 2 :])
+
+
+def ring_gather(x, axis, dim):
+    size = lax.axis_size(axis)
+    pairs = [(i, (i + 1) % size) for i in range(size)]
+    back = [(b, a) for a, b in pairs]
+    lower, upper = ([], [])
+    for lap in range(size - 1):
+        if lap % 2 == 0:
+            lower.append(lax.ppermute(lower[-1] if lower else x, axis, pairs))
+        else:
+            upper.append(lax.ppermute(upper[-1] if upper else x, axis, back))
+    tiles = jnp.stack([*lower[::-1], x, *upper])
+    shift = lax.axis_index(axis) - len(lower)
+    tiles = tiles[(jnp.arange(size) - shift) % size]
+    return joined_along(tiles, dim)
 
 
 def layer_norm(values, gain, shift):
@@ -59,7 +81,7 @@
     tp_count = lax.axis_size("tensor")
     w_proj_all = lax.all_gather(w_proj, "dp", axis=0, tiled=True)
     w_out_all = lax.all_gather(w_out, "tensor", axis=0, tiled=True)
-    gathered = lax.all_gather(tokens, "tensor", axis=0, tiled=True)
+    gathered = ring_gather(tokens, "tensor", 0)
     row_count = gathered.shape[0]
     local_rows = tokens.shape[0]
     normed = layer_norm(gathered, ln1_gain, ln1_shift).astype(jnp.bfloat16)

time: 340 us -> 304 us (0.89)
  waiting for transfers between devices: 226 us -> 169 us
  local copies, waits for them, and re-layouts: 5.09 us -> 20.4 us
  starting transfers between devices: 0.12 us -> 9.36 us
  blocking collectives: 63.7 us -> 58.7 us
    all_gather x1, waiting for transfers between devices: 147 us -> 107 us  [shards(): w_proj_all = lax.all_gather(w_proj, 'dp', axis=0, tiled=True)]
    all_gather x1 -> x0, waiting for transfers between devices: 36.8 us -> none  [shards(): gathered = lax.all_gather(tokens, 'tensor', axis=0, tiled=True)]
    ppermute x0 -> x7, waiting for transfers between devices: none -> 28.2 us  [the longest x4 23.8 us: ring_gather(): lower.append(lax.ppermute(lower[-1] if lower else x, axis, pairs))]
    unnamed x23 -> x30, local copies, waits for them, and re-layouts: 0.76 us -> 10.9 us
    ppermute x0 -> x7, starting transfers between devices: none -> 9.29 us  [the longest x3 9.26 us: ring_gather(): upper.append(lax.ppermute(upper[-1] if upper else x, axis, back))]
    all_gather x1, waiting for transfers between devices: 8.44 us -> 0.01 us  [shards(): w_out_all = lax.all_gather(w_out, 'tensor', axis=0, tiled=True)]
    all_to_all x1, blocking collectives: 16 us -> 11 us  [shards(): lax.all_to_all(context, 'tensor', split_axis=0, concat_axis=0, tiled=True)]
    gather x0 -> x1, local copies, waits for them, and re-layouts: none -> 4.33 us  [ring_gather(): tiles = tiles[(jnp.arange(size) - shift) % size]]
  transfers between devices with their start and end apart: 4 -> 10, of which waited for: 4 -> 7; matrix products, arithmetic and copies ran while one was open for 8% -> 15% of each run, Pallas kernels for 0% -> 0%
where the time goes in v1:
time: 304 us
  waiting for transfers between devices  169 us (56%)
  blocking collectives  58.7 us (19%)
  matrix products  26.6 us (9%)
  local copies, waits for them, and re-layouts  20.4 us (7%)
  between operations  13.3 us (4%)
  starting transfers between devices  9.36 us (3%)
  other arithmetic  6.34 us (2%)
    all_gather x1, waiting for transfers between devices, shards(): w_proj_all = lax.all_gather(w_proj, 'dp', axis=0, tiled=True)  107 us
    all_to_all x1, blocking collectives, shards(): lax.all_to_all(outgoing, 'dp', split_axis=0, concat_axis=0, tiled=True)  47.7 us
    all_gather x1, waiting for transfers between devices, shards(): merged = lax.all_gather(merged_mine, 'tensor', axis=0, tiled=True)  32.6 us
    ppermute x4, waiting for transfers between devices, ring_gather(): lower.append(lax.ppermute(lower[-1] if lower else x, axis, pairs))  23.8 us
    all_to_all x1, blocking collectives, shards(): lax.all_to_all(context, 'tensor', split_axis=0, concat_axis=0, tiled=True)  11 us
    unnamed x30, local copies, waits for them, and re-layouts  10.9 us
    sub x2, matrix products, attend(): exponent = jnp.exp(scores - row_max)  9.54 us
    ppermute x3, starting transfers between devices, ring_gather(): upper.append(lax.ppermute(upper[-1] if upper else x, axis, back))  9.26 us
  transfers between devices with their start and end apart: 10, of which 7 were waited for; matrix products, arithmetic and copies ran while one was open for 15% of the time, Pallas kernels for 0%

profile of v1, /device:TPU:8, one launch (start us, length us, event | category | flops | bytes accessed | tf_op | source)
XLA Modules:
  0.0 303.7 jit_solution(14895337908173008195)
XLA Ops:
  6.5 0.0 copy-start
  6.5 0.7 all-gather.4.cloned.1.call-update
  7.3 0.0 all-gather.8.cloned.1.call-start
  7.3 0.0 collective-permute-start
  7.3 8.3 %collective-permute-done = bf16[128,1408]{1,0:T(8,128)(2,1)S(1)} collective-permute-done((bf16[128,1408]{1,0:T(8,128)(2,1)}, bf16[128,1408]{1,0:T(8,128)(2,1)S(1)}, u32[]{:S(2)}, u32[]{:S(2)}) %collective-permute-start) | collective-permute-done | bytes 360480 | tf_op jit(solution)/shard_map/ppermute | solution.py:20
  15.6 0.0 collective-permute-start.1
  15.6 3.0 collective-permute-start.4
  18.5 5.1 %collective-permute-done.1 = bf16[128,1408]{1,0:T(8,128)(2,1)S(1)} collective-permute-done((bf16[128,1408]{1,0:T(8,128)(2,1)S(1)}, bf16[128,1408]{1,0:T(8,128)(2,1)S(1)}, u32[]{:S(2)}, u32[]{:S(2)}) %collective-permute-start.1) | collective-permute-done | bytes 360480 | tf_op jit(solution)/shard_map/ppermute | solution.py:20
  23.7 0.0 collective-permute-start.2
  23.7 0.0 all-gather.8.cloned.1.call-update
  23.7 0.0 all-gather.6.cloned.1.call-start
  23.7 0.7 slice_bitcast_fusion.1
  24.5 0.1 broadcast_in_dim.24
  24.5 0.1 eq.86
  24.7 0.1 broadcast_in_dim.28
  24.7 0.1 eq.91
  24.9 0.8 broadcast_in_dim.25
  25.6 0.1 eq.88
  25.8 0.0 collective-permute-done.4
  25.8 2.9 collective-permute-start.5
  28.7 3.2 %collective-permute-done.2 = bf16[128,1408]{1,0:T(8,128)(2,1)} collective-permute-done((bf16[128,1408]{1,0:T(8,128)(2,1)S(1)}, bf16[128,1408]{1,0:T(8,128)(2,1)}, u32[]{:S(2)}, u32[]{:S(2)}) %collective-permute-start.2) | collective-permute-done | bytes 360480 | tf_op jit(solution)/shard_map/ppermute | solution.py:20
  31.8 0.0 collective-permute-start.3
  31.8 0.7 broadcast_compare_fusion.1
  32.5 4.4 %collective-permute-done.5 = bf16[128,1408]{1,0:T(8,128)(2,1)} collective-permute-done((bf16[128,1408]{1,0:T(8,128)(2,1)}, bf16[128,1408]{1,0:T(8,128)(2,1)}, u32[]{:S(2)}, u32[]{:S(2)}) %collective-permute-start.5) | collective-permute-done | bytes 360480 | tf_op jit(solution)/shard_map/ppermute | solution.py:22
  36.9 3.4 %collective-permute-start.6 = (bf16[128,1408]{1,0:T(8,128)(2,1)}, bf16[128,1408]{1,0:T(8,128)(2,1)S(1)}, u32[]{:S(2)}, u32[]{:S(2)}) collective-permute-start(bf16[128,1408]{1,0:T(8,128)(2,1)} %collective-permute-done.5), channel_id=1, source_target_pairs={{1,0},{2,1},{3,2},{4,3},{5,4},{6,5},{7,6},{0,7},{9,8},{10,9},{11,1... | collective-permute-start | bytes 1081352 | tf_op jit(solution)/shard_map/ppermute | solution.py:22
  40.3 7.3 %collective-permute-done.3 = bf16[128,1408]{1,0:T(8,128)(2,1)} collective-permute-done((bf16[128,1408]{1,0:T(8,128)(2,1)}, bf16[128,1408]{1,0:T(8,128)(2,1)}, u32[]{:S(2)}, u32[]{:S(2)}) %collective-permute-start.3) | collective-permute-done | bytes 360480 | tf_op jit(solution)/shard_map/ppermute | solution.py:20
  47.6 1.8 bitcast_dynamic-update-slice_fusion.7
  49.4 1.7 bitcast_dynamic-update-slice_fusion.6
  51.1 1.8 bitcast_dynamic-update-slice_fusion.5
  52.9 0.8 bitcast_dynamic-update-slice_fusion.4
  53.7 0.8 bitcast_dynamic-update-slice_fusion.3
  54.4 1.7 bitcast_dynamic-update-slice_fusion.2
  56.2 1.7 bitcast_dynamic-update-slice_fusion.1
  57.9 0.0 collective-permute-done.6
  57.9 0.8 bitcast_dynamic-update-slice_fusion
  58.7 4.3 %gather_fusion = bf16[8,128,1408]{2,1,0:T(8,128)(2,1)} fusion(bf16[8,128,1408]{2,1,0:T(8,128)(2,1)} %bitcast_dynamic-update-slice_fusion, s32[1024]{0:T(1024)S(1)} %pad_clamp_fusion), kind=kCustom, calls=%fused_computation | custom fusion | bytes 5767200 | tf_op jit(solution)/shard_map/gather | solution.py:25
  63.1 2.4 convert_reduce_fusion
  65.5 0.3 copy-done.1
  65.7 0.9 fusion.4
  66.7 1.1 fusion.7
  67.8 0.0 copy-done
  67.8 2.9 convolution_convert_fusion
  70.7 4.8 %fusion.75 = (f32[2,512]{1,0:T(2,128)S(1)}, f32[2,512,1024]{2,1,0:T(8,128)}) fusion(pred[512,1024]{1,0:T(8,128)(4,1)S(1)} %get-tuple-element.5, bf16[1024,2,264]{0,2,1:T(8,128)(2,1)} %bitcast.84), kind=kOutput, calls=%fused_computation.97 | convolution fusion | flops 188744704 | bytes 5263360 | tf_op jit(solution)/shard_map/sub | solution.py:60
  75.5 4.7 %fusion.66 = (f32[2,512]{1,0:T(2,128)S(1)}, f32[2,512,1024]{2,1,0:T(8,128)}) fusion(pred[512,1024]{1,0:T(8,128)(4,1)S(1)} %get-tuple-element.6, bf16[1024,2,264]{0,2,1:T(8,128)(2,1)} %bitcast.85), kind=kOutput, calls=%fused_computation.96 | convolution fusion | flops 188744704 | bytes 5263360 | tf_op jit(solution)/shard_map/sub | solution.py:60
  80.3 3.3 %fusion.24 = bf16[512,2,88]{0,2,1:T(8,128)(2,1)S(1)} fusion(f32[2,512,1024]{2,1,0:T(8,128)} %get-tuple-element.12, f32[2,512]{1,0:T(2,128)S(1)} %get-tuple-element.11, bf16[1024,2,264]{0,2,1:T(8,128)(2,1)} %bitcast.86), kind=kOutput, calls=%fused_computation.37 | convolution fusion | flops 186736640 | bytes 4739072 | tf_op jit(solution)/shard_map/hqk,khd->qhd/dot_general | solution.py:62
  83.5 0.3 copy-done.10
  83.8 1.9 fusion.25
  85.7 0.1 copy.22
  85.9 11.0 %all_to_all.10 = bf16[8,128,176]{1,2,0:T(8,128)(2,1)S(1)} all-to-all(bf16[8,128,176]{1,2,0:T(8,128)(2,1)S(1)} %copy.18), channel_id=1, replica_groups=mesh['dp'=64,'tensor'=8] {'tensor'}, dimensions={0} | all-to-all | bytes 720896 | tf_op jit(solution)/shard_map/all_to_all | solution.py:95
  96.8 3.1 %fusion.84 = (f32[128]{0:T(128)S(1)}, f32[128,1408]{1,0:T(8,128)S(1)}) fusion(bf16[8,128,176]{1,2,0:T(8,128)(2,1)S(1)} %all_to_all.10, bf16[8,176,1408]{2,1,0:T(8,128)(2,1)} %bitcast.74, bf16[128,1408]{1,0:T(8,128)(2,1)S(1)} %copy-done.2), kind=kOutput, calls=%fused_computation.98 | convolution fusion | flops 508411776 | bytes 5407232 | tf_op jit(solution)/shard_map/sqd,sdo->qo/dot_general | solution.py:97
  99.9 0.0 copy-start.9
  99.9 0.2 multiply_reduce_fusion
  100.2 0.2 add_convert_fusion
  100.4 1.0 reshape.303
  101.4 0.0 all-gather.6.cloned.1.call-update
  101.4 0.6 reduce-window.6
  102.0 0.2 slice_reduce_fusion
  102.3 0.1 fusion.58
  102.4 107.3 %all-gather.8.cloned.1.call-done = bf16[5632,448]{1,0:T(8,128)(2,1)} async-done(((bf16[88,448]{1,0:T(8,128)(2,1)}), bf16[5632,448]{1,0:T(8,128)(2,1)}) %all-gather.8.cloned.1.call-update) | async-done | bytes 5046288 | tf_op jit(solution)/shard_map/all_gather | solution.py:82
  209.7 32.6 %all-gather.6.cloned.1.call-done = bf16[256,5632]{1,0:T(8,128)(2,1)} async-done(((bf16[32,5632]{1,0:T(8,128)(2,1)}), bf16[256,5632]{1,0:T(8,128)(2,1)}) %all-gather.6.cloned.1.call-update) | async-done | bytes 2883600 | tf_op jit(solution)/shard_map/all_gather | solution.py:101
  242.3 6.0 %convolution_convert_fusion.1 = bf16[512,448]{0,1:T(8,128)(2,1)S(1)} fusion(bf16[256,5632]{1,0:T(8,128)(2,1)} %all-gather.6.cloned.1.call-done, bf16[5632,448]{1,0:T(8,128)(2,1)} %all-gather.8.cloned.1.call-done, s32[256]{0:T(256)S(1)} %multiply_add_fusion, f32[448]{0:T(512)S(1)} %copy-done.9), kind=kOutput, calls=%fused_computation.32 | convolution fusion | flops 1409875968 | bytes 8391424 | tf_op jit(solution)/shard_map/dot_general | solution.py:114
  248.3 0.2 copy.19
  248.5 47.7 %all_to_all.11 = bf16[64,8,448]{2,1,0:T(8,128)(2,1)S(1)} all-to-all(bf16[64,8,448]{2,1,0:T(8,128)(2,1)S(1)} %bitcast.76), channel_id=1, replica_groups=mesh['dp'=64,'tensor'=8] {'dp'}, dimensions={0} | all-to-all | bytes 917504 | tf_op jit(solution)/shard_map/all_to_all | solution.py:118
  296.3 1.0 copy.20
  (31 shorter events, 0.2 us)
Async XLA Ops:
  6.5 61.3 %copy-start = (bf16[1408,2,264]{0,2,1:T(8,128)(2,1)S(1)}, bf16[1408,2,264]{0,2,1:T(8,128)(2,1)}, u32[]{:S(2)}) copy-start(bf16[1408,2,264]{0,2,1:T(8,128)(2,1)} %param.14) | copy-start | bytes 4460548
  6.5 47.1 %copy-start.2 = (bf16[128,1408]{1,0:T(8,128)(2,1)S(1)}, bf16[128,1408]{1,0:T(8,128)(2,1)}, u32[]{:S(2)}) copy-start(bf16[128,1408]{1,0:T(8,128)(2,1)} %param.11) | copy-start | bytes 1081348
  6.5 90.3 %all-gather.4.cloned.1.call-start = ((), (), s32[]{:S(2)}) async-start(), calls=%async_computation.2 | async-start | bytes 4460544 | tf_op jit(solution)/shard_map/all_gather | solution.py:83
  7.3 202.4 %all-gather.8.cloned.1.call-start = ((), (), s32[]{:S(2)}) async-start(), calls=%async_computation.4 | async-start | bytes 5857280 | tf_op jit(solution)/shard_map/all_gather | solution.py:82
  7.3 8.3 %collective-permute-start = (bf16[128,1408]{1,0:T(8,128)(2,1)}, bf16[128,1408]{1,0:T(8,128)(2,1)S(1)}, u32[]{:S(2)}, u32[]{:S(2)}) collective-permute-start(bf16[128,1408]{1,0:T(8,128)(2,1)} %param.11), channel_id=1, source_target_pairs={{0,1},{1,2},{2,3},{3,4},{4,5},{5,6},{6,7},{7,0},{8,9},{9,10},{10,1... | collective-permute-start | bytes 1081352 | tf_op jit(solution)/shard_map/ppermute | solution.py:20
  15.6 8.1 %collective-permute-start.1 = (bf16[128,1408]{1,0:T(8,128)(2,1)S(1)}, bf16[128,1408]{1,0:T(8,128)(2,1)S(1)}, u32[]{:S(2)}, u32[]{:S(2)}) collective-permute-start(bf16[128,1408]{1,0:T(8,128)(2,1)S(1)} %collective-permute-done), channel_id=1, source_target_pairs={{0,1},{1,2},{2,3},{3,4},{4,5},{5,6},{6,7},{7,0},{8,9},{9,10},{10,1... | collective-permute-start | bytes 1081352 | tf_op jit(solution)/shard_map/ppermute | solution.py:20
  15.6 10.2 %collective-permute-start.4 = (bf16[128,1408]{1,0:T(8,128)(2,1)}, bf16[128,1408]{1,0:T(8,128)(2,1)}, u32[]{:S(2)}, u32[]{:S(2)}) collective-permute-start(bf16[128,1408]{1,0:T(8,128)(2,1)} %param.11), channel_id=1, source_target_pairs={{1,0},{2,1},{3,2},{4,3},{5,4},{6,5},{7,6},{0,7},{9,8},{10,9},{11,1... | collective-permute-start | bytes 1081352 | tf_op jit(solution)/shard_map/ppermute | solution.py:22
  23.7 8.2 %copy-start.3 = (bf16[128,1408]{1,0:T(8,128)(2,1)}, bf16[128,1408]{1,0:T(8,128)(2,1)S(1)}, u32[]{:S(2)}) copy-start(bf16[128,1408]{1,0:T(8,128)(2,1)S(1)} %collective-permute-done.1) | copy-start | bytes 1081348
  23.7 8.2 %collective-permute-start.2 = (bf16[128,1408]{1,0:T(8,128)(2,1)S(1)}, bf16[128,1408]{1,0:T(8,128)(2,1)}, u32[]{:S(2)}, u32[]{:S(2)}) collective-permute-start(bf16[128,1408]{1,0:T(8,128)(2,1)S(1)} %collective-permute-done.1), channel_id=1, source_target_pairs={{0,1},{1,2},{2,3},{3,4},{4,5},{5,6},{6,7},{7,0},{8,9},{9,10},{10,1... | collective-permute-start | bytes 1081352 | tf_op jit(solution)/shard_map/ppermute | solution.py:20
  23.7 218.6 %all-gather.6.cloned.1.call-start = ((), (), s32[]{:S(2)}) async-start(), calls=%async_computation.3 | async-start | bytes 3244032 | tf_op jit(solution)/shard_map/all_gather | solution.py:101
  25.8 11.2 %collective-permute-start.5 = (bf16[128,1408]{1,0:T(8,128)(2,1)}, bf16[128,1408]{1,0:T(8,128)(2,1)}, u32[]{:S(2)}, u32[]{:S(2)}) collective-permute-start(bf16[128,1408]{1,0:T(8,128)(2,1)} %collective-permute-done.4), channel_id=1, source_target_pairs={{1,0},{2,1},{3,2},{4,3},{5,4},{6,5},{7,6},{0,7},{9,8},{10,9},{11,1... | collective-permute-start | bytes 1081352 | tf_op jit(solution)/shard_map/ppermute | solution.py:22
  31.8 15.8 %collective-permute-start.3 = (bf16[128,1408]{1,0:T(8,128)(2,1)}, bf16[128,1408]{1,0:T(8,128)(2,1)}, u32[]{:S(2)}, u32[]{:S(2)}) collective-permute-start(bf16[128,1408]{1,0:T(8,128)(2,1)} %collective-permute-done.2), channel_id=1, source_target_pairs={{0,1},{1,2},{2,3},{3,4},{4,5},{5,6},{6,7},{7,0},{8,9},{9,10},{10,1... | collective-permute-start | bytes 1081352 | tf_op jit(solution)/shard_map/ppermute | solution.py:20
  36.9 21.0 %collective-permute-start.6 = (bf16[128,1408]{1,0:T(8,128)(2,1)}, bf16[128,1408]{1,0:T(8,128)(2,1)S(1)}, u32[]{:S(2)}, u32[]{:S(2)}) collective-permute-start(bf16[128,1408]{1,0:T(8,128)(2,1)} %collective-permute-done.5), channel_id=1, source_target_pairs={{1,0},{2,1},{3,2},{4,3},{5,4},{6,5},{7,6},{0,7},{9,8},{10,9},{11,1... | collective-permute-start | bytes 1081352 | tf_op jit(solution)/shard_map/ppermute | solution.py:22
  63.1 2.7 copy-start.1
  63.1 3.6 %copy-start.5 = (f32[1408]{0:T(1024)S(1)}, f32[1408]{0:T(1024)}, u32[]{:S(2)}) copy-start(f32[1408]{0:T(1024)} %param.13) | copy-start | bytes 16900
  63.1 3.6 %copy-start.6 = (f32[1408]{0:T(1024)S(1)}, f32[1408]{0:T(1024)}, u32[]{:S(2)}) copy-start(f32[1408]{0:T(1024)} %param.12) | copy-start | bytes 16900
  80.3 3.6 %copy-start.10 = (f32[2,512,1024]{2,1,0:T(8,128)S(1)}, f32[2,512,1024]{2,1,0:T(8,128)}, u32[]{:S(2)}) copy-start(f32[2,512,1024]{2,1,0:T(8,128)} %get-tuple-element.10) | copy-start | bytes 12582916
  96.8 3.3 %copy-start.7 = (f32[1408]{0:T(1024)S(1)}, f32[1408]{0:T(1024)}, u32[]{:S(2)}) copy-start(f32[1408]{0:T(1024)} %param.17) | copy-start | bytes 16900
  96.8 3.3 %copy-start.8 = (f32[1408]{0:T(1024)S(1)}, f32[1408]{0:T(1024)}, u32[]{:S(2)}) copy-start(f32[1408]{0:T(1024)} %param.16) | copy-start | bytes 16900
  96.8 4.6 %copy-start.4 = (s32[256,1]{0,1:T(1,128)S(1)}, s32[256,1]{0,1:T(1,128)}, u32[]{:S(2)}) copy-start(s32[256,1]{0,1:T(1,128)} %param.21) | copy-start | bytes 3076
  99.9 142.4 %copy-start.9 = (f32[448]{0:T(512)S(1)}, f32[448]{0:T(512)}, u32[]{:S(2)}) copy-start(f32[448]{0:T(512)} %param.19) | copy-start | bytes 5380
Sparse Core Ops, SparseCore 0:
  9.5 47.0 all-gather.3
  59.5 150.1 all-gather.7
  211.8 30.4 all-gather.5
